TPU v7x, 512 devices: a whole 4x4x16 slice. The times are simulated.
512 devices in a mesh: dp: 16 (over x, y), seq: 32 (over z, core).
Axes of the slice: x: 4, y: 4, z: 16, core: 2. Of those that a mesh axis runs over, the one named last changes fastest.
Arguments:
- query_rows: bfloat16 [32, 2048, 2048], P('seq', 'dp'), may hold values from -8 to 8
- key_rows: bfloat16 [32, 2048, 2048], P('seq', 'dp'), may hold values from -8 to 8
- value_rows: bfloat16 [32, 2048, 2048], P('seq', 'dp'), may hold values from -6 to 6
- out_grad: bfloat16 [32, 2048, 3072], P('seq', 'dp'), may hold values from -96 to 96
- out_weight: bfloat16 [2, 2048, 3072], P(None, ('dp', 'seq')), may hold values from -0.125 to 0.125
- text_length: int32 [32], P('seq'), may hold values from 65 to 512
Outputs:
- query_grad: bfloat16 [32, 2048, 2048], P('seq', 'dp')
- key_grad: bfloat16 [32, 2048, 2048], P('seq', 'dp')
- value_grad: bfloat16 [32, 2048, 2048], P('seq', 'dp')
All inputs are finite; a program needn't handle non-finite values.
Results may differ from a plain program's by a relative error of at most 0.0076.
Values may be sent and summed in bfloat16 or wider, within the bound.
No kernel may reach another device: no remote copies, remote signals or barrier semaphores. Data moves between devices by JAX's collectives and lax.ppermute only.
A program may use at most 128 MiB of HBM per device.

v0:
```python
import math
import jax
import jax.numpy as jnp
from jax import lax
from jax.sharding import PartitionSpec as P

HEADS = 16
HEAD_DIM = 128
TXT = 512


def attention_grads(query_heads, key_heads, value_heads, grad_heads, key_valid):
    total_rows = query_heads.shape[0]
    block_rows = min(512, total_rows)
    factor = 1.0 / math.sqrt(query_heads.shape[2])
    key_total = jnp.zeros(key_heads.shape, jnp.float32)
    value_total = jnp.zeros(value_heads.shape, jnp.float32)
    query_parts = []
    for first_row in range(0, total_rows, block_rows):
        query_block = query_heads[first_row : first_row + block_rows]
        grad_block = grad_heads[first_row : first_row + block_rows]
        scores = (
            jnp.einsum("qhc,khc->hqk", query_block, key_heads, preferred_element_type=jnp.float32)
            * factor
        )
        scores = jnp.where(key_valid[None, None, :], scores, -jnp.inf)
        shifted = jnp.exp(scores - jnp.max(scores, axis=2, keepdims=True))
        attention = shifted / jnp.sum(shifted, axis=2, keepdims=True)
        value_total = value_total + jnp.einsum(
            "hqk,qhc->khc",
            attention.astype(jnp.bfloat16),
            grad_block,
            preferred_element_type=jnp.float32,
        )
        weight_grad = jnp.einsum(
            "qhc,khc->hqk", grad_block, value_heads, preferred_element_type=jnp.float32
        )
        row_dot = jnp.sum(attention * weight_grad, axis=2, keepdims=True)
        score_grad = (attention * (weight_grad - row_dot) * factor).astype(jnp.bfloat16)
        query_parts.append(
            jnp.einsum(
                "hqk,khc->qhc", score_grad, key_heads, preferred_element_type=jnp.float32
            ).astype(jnp.bfloat16)
        )
        key_total = key_total + jnp.einsum(
            "hqk,qhc->khc", score_grad, query_block, preferred_element_type=jnp.float32
        )
    return (
        jnp.concatenate(query_parts, axis=0),
        key_total.astype(jnp.bfloat16),
        value_total.astype(jnp.bfloat16),
    )


def per_device(query_rows, key_rows, value_rows, out_grad, out_weight, text_length):
    devices = lax.axis_size("dp")
    tok_rows = query_rows.shape[1]
    total_rows = tok_rows * devices
    positions = jnp.arange(total_rows)
    key_valid = (positions >= TXT) | (positions < text_length[0])

    def by_heads(array):
        return array[0].reshape(tok_rows, HEADS, HEAD_DIM)

    slot_text = (jnp.arange(devices) * tok_rows < TXT)[:, None, None]
    outgoing = jnp.where(slot_text, out_weight[0][None], out_weight[1][None])
    stream_rows = lax.all_to_all(outgoing, "dp", split_axis=0, concat_axis=0, tiled=True)
    projected = jnp.einsum(
        "te,kre->tkr",
        out_grad[0],
        lax.all_gather(stream_rows, "seq", axis=1, tiled=True),
        preferred_element_type=jnp.float32,
    )
    grad_tokens = projected.astype(jnp.bfloat16)
    query_heads, key_heads, value_heads, grad_heads = (
        lax.all_to_all(by_heads(query_rows), "dp", split_axis=1, concat_axis=0, tiled=True),
        lax.all_to_all(by_heads(key_rows), "dp", split_axis=1, concat_axis=0, tiled=True),
        lax.all_to_all(by_heads(value_rows), "dp", split_axis=1, concat_axis=0, tiled=True),
        lax.all_to_all(grad_tokens, "dp", split_axis=1, concat_axis=0, tiled=True),
    )
    query_grad, key_grad, value_grad = attention_grads(
        query_heads, key_heads, value_heads, grad_heads, key_valid
    )
    returned = (
        lax.all_to_all(query_grad, "dp", split_axis=0, concat_axis=1, tiled=True),
        lax.all_to_all(key_grad, "dp", split_axis=0, concat_axis=1, tiled=True),
        lax.all_to_all(value_grad, "dp", split_axis=0, concat_axis=1, tiled=True),
    )
    return (
        returned[0].reshape(1, tok_rows, HEADS * HEAD_DIM),
        returned[1].reshape(1, tok_rows, HEADS * HEAD_DIM),
        returned[2].reshape(1, tok_rows, HEADS * HEAD_DIM),
    )


def solution(mesh):
    in_specs = (
        P("seq", "dp", None),
        P("seq", "dp", None),
        P("seq", "dp", None),
        P("seq", "dp", None),
        P(None, ("dp", "seq"), None),
        P("seq"),
    )
    out_specs = (P("seq", "dp", None), P("seq", "dp", None), P("seq", "dp", None))
    return jax.shard_map(
        per_device, mesh=mesh, in_specs=in_specs, out_specs=out_specs, check_vma=False
    )
```

profile of v0, /device:TPU:32, one launch (start us, length us, event | category | flops | bytes accessed | tf_op | source)
XLA Modules:
  0.0 236.3 jit_solution(1114282494881835689)
XLA Ops:
  8.4 16.7 %all_to_all.110 = bf16[16,4,3072]{2,1,0:T(4,128)(2,1)S(1)} all-to-all(bf16[16,4,3072]{2,1,0:T(4,128)(2,1)S(1)} %broadcast_select_fusion), channel_id=1, replica_groups=mesh['dp'=16,'seq'=32] {'dp'}, dimensions={0} | all-to-all | bytes 786432 | tf_op jit(solution)/shard_map/all_to_all | solution.py:67
  28.0 3.7 %all-to-all-start = ((bf16[128,16,128]{0,2,1:T(8,128)(2,1)}), bf16[128,16,128]{0,2,1:T(8,128)(2,1)S(1)}, u32[]{:S(2)}, u32[]{:S(2)}) async-start(bf16[128,16,128]{0,2,1:T(8,128)(2,1)} %bitcast.1), calls=%async_computation | async-start | bytes 1048576 | tf_op jit(solution)/shard_map/all_to_all | solution.py:76
  32.7 9.3 %all-to-all-done = bf16[128,16,128]{0,2,1:T(8,128)(2,1)S(1)} async-done(((bf16[128,16,128]{0,2,1:T(8,128)(2,1)}), bf16[128,16,128]{0,2,1:T(8,128)(2,1)S(1)}, u32[]{:S(2)}, u32[]{:S(2)}) %all-to-all-start) | async-done | bytes 524320 | tf_op jit(solution)/shard_map/all_to_all | solution.py:76
  42.0 3.6 %all-to-all-start.1 = ((bf16[128,16,128]{0,2,1:T(8,128)(2,1)}), bf16[128,16,128]{0,2,1:T(8,128)(2,1)S(1)}, u32[]{:S(2)}, u32[]{:S(2)}) async-start(bf16[128,16,128]{0,2,1:T(8,128)(2,1)} %bitcast.5), calls=%async_computation.1 | async-start | bytes 1048576 | tf_op jit(solution)/shard_map/all_to_all | solution.py:77
  47.9 7.8 %all-to-all-done.1 = bf16[128,16,128]{0,2,1:T(8,128)(2,1)S(1)} async-done(((bf16[128,16,128]{0,2,1:T(8,128)(2,1)}), bf16[128,16,128]{0,2,1:T(8,128)(2,1)S(1)}, u32[]{:S(2)}, u32[]{:S(2)}) %all-to-all-start.1) | async-done | bytes 524320 | tf_op jit(solution)/shard_map/all_to_all | solution.py:77
  55.7 3.6 %all-to-all-start.4 = ((bf16[128,16,128]{0,2,1:T(8,128)(2,1)}), bf16[128,16,128]{0,2,1:T(8,128)(2,1)S(1)}, u32[]{:S(2)}, u32[]{:S(2)}) async-start(bf16[128,16,128]{0,2,1:T(8,128)(2,1)} %bitcast.17), calls=%async_computation.4 | async-start | bytes 1048576 | tf_op jit(solution)/shard_map/all_to_all | solution.py:78
  67.6 45.6 %all-gather.2.cloned.1.call-done = bf16[16,128,3072]{2,0,1:T(8,128)(2,1)} async-done(((bf16[16,4,3072]{2,0,1:T(8,128)(2,1)}), bf16[16,128,3072]{2,0,1:T(8,128)(2,1)}) %all-gather.2.cloned.1.call-update) | async-done | bytes 12582928 | tf_op jit(solution)/shard_map/all_gather | solution.py:71
  113.2 6.5 %fusion.21 = bf16[128,16,128]{0,1,2:T(8,128)(2,1)S(1)} fusion(bf16[16,128,3072]{2,0,1:T(8,128)(2,1)} %all-gather.2.cloned.1.call-done, bf16[1,128,3072]{2,1,0:T(8,128)(2,1)S(1)} %copy-done), kind=kOutput, calls=%fused_computation.44 | convolution fusion | flops 1610874880 | bytes 13893632 | tf_op jit(solution)/shard_map/te,kre->tkr/dot_general | solution.py:68
  120.6 7.0 %all-to-all-start.3 = ((bf16[128,16,128]{0,2,1:T(8,128)(2,1)}), bf16[128,16,128]{0,2,1:T(8,128)(2,1)S(1)}, u32[]{:S(2)}, u32[]{:S(2)}) async-start(bf16[128,16,128]{0,2,1:T(8,128)(2,1)} %copy.98), calls=%async_computation.3 | async-start | bytes 1048576 | tf_op jit(solution)/shard_map/all_to_all | solution.py:79
  130.5 3.1 %fusion.5 = f32[512]{0:T(512)S(1)} fusion(f32[512,2048]{1,0:T(8,128)} %get-tuple-element.33, f32[512]{0:T(512)S(1)} %get-tuple-element.32, pred[2048]{0:T(1024)(128)(4,1)S(1)} %fusion.27), kind=kLoop, calls=%fused_computation.21 | loop fusion | flops 4193792 | bytes 4200448 | tf_op jit(solution)/shard_map/reduce_sum | solution.py:28
  133.7 5.8 %all-to-all-done.3 = bf16[128,16,128]{0,2,1:T(8,128)(2,1)S(1)} async-done(((bf16[128,16,128]{0,2,1:T(8,128)(2,1)}), bf16[128,16,128]{0,2,1:T(8,128)(2,1)S(1)}, u32[]{:S(2)}, u32[]{:S(2)}) %all-to-all-start.3) | async-done | bytes 524320 | tf_op jit(solution)/shard_map/all_to_all | solution.py:79
  140.6 3.0 %copy-done.2 = f32[512,2048]{1,0:T(8,128)S(1)} copy-done((f32[512,2048]{1,0:T(8,128)S(1)}, f32[512,2048]{1,0:T(8,128)}, u32[]{:S(2)}) %copy-start.2) | copy-done | bytes 4194328
  148.6 3.9 %multiply_reduce_fusion.3 = (f32[512]{0:T(512)S(1)}, f32[512]{0:T(512)S(1)}, f32[512]{0:T(512)S(1)}, f32[512]{0:T(512)S(1)}, f32[512,2048]{1,0:T(8,128)}) fusion(f32[512]{0:T(512)S(1)} %fusion.5, f32[512]{0:T(512)S(1)} %get-tuple-element.32, f32[512,2048]{1,0:T(8,128)S(1)} %copy-done.2, pred[2048]{0:T(1024)(128)(4,1)S(1)} %fusion.27, ...), kind=kOutput, calls=%fused_computation.13 | convolution fusion | flops 284162048 | bytes 21641216 | tf_op jit(solution)/shard_map/qhc,khc->hqk/dot_general | solution.py:35
  153.4 4.5 %multiply_reduce_fusion.2 = (f32[512]{0:T(512)S(1)}, f32[512]{0:T(512)S(1)}, f32[512]{0:T(512)S(1)}, f32[512,2048]{1,0:T(8,128)}) fusion(f32[512]{0:T(512)S(1)} %fusion.7, f32[512]{0:T(512)S(1)} %get-tuple-element.10, f32[512,2048]{1,0:T(8,128)S(1)} %copy-done.3, pred[2048]{0:T(1024)(128)(4,1)S(1)} %fusion.27, f32[512]{0:T(512)S(1)} %get-tuple-element.11, ...), kind=kOutput, calls=%fused_computation.9 | convolution fusion | flops 283113984 | bytes 17448960 | tf_op jit(solution)/shard_map/qhc,khc->hqk/dot_general | solution.py:35
  157.9 7.4 %multiply_reduce_fusion.1 = (f32[512]{0:T(512)S(1)}, f32[512]{0:T(512)S(1)}, bf16[512,2048]{1,0:T(8,128)(2,1)}, f32[512,2048]{1,0:T(8,128)}) fusion(f32[512]{0:T(512)S(1)} %get-tuple-element.14, f32[512]{0:T(512)S(1)} %get-tuple-element.11, f32[512,2048]{1,0:T(8,128)S(1)} %copy-done.5, pred[2048]{0:T(1024)(128)(4,1)S(1)} %fusion.27, ...), kind=kOutput, calls=%fused_computation.5 | convolution fusion | flops 289405952 | bytes 27938816 | tf_op jit(solution)/shard_map/qhc,khc->hqk/dot_general | solution.py:35
  165.3 8.2 %multiply_convert_fusion.3 = (bf16[512,2048]{1,0:T(8,128)(2,1)S(1)}, bf16[512,2048]{1,0:T(8,128)(2,1)S(1)}, bf16[512,2048]{1,0:T(8,128)(2,1)S(1)}) fusion(f32[512,2048]{1,0:T(8,128)} %get-tuple-element.34, f32[512]{0:T(512)S(1)} %get-tuple-element.9, f32[512]{0:T(512)S(1)} %fusion.5, f32[512]{0:T(512)S(1)} %get-tuple-element.32, ...), kind=kLoop, calls=%fused_computation.12 | loop fusion | flops 25165824 | bytes 31477760 | tf_op jit(solution)/shard_map/convert_element_type | solution.py:39
  186.0 3.6 %all-to-all-start.5 = ((bf16[16,2,8192]{2,1,0:T(2,128)(2,1)}), bf16[16,2,8192]{2,1,0:T(2,128)(2,1)S(1)}, u32[]{:S(2)}, u32[]{:S(2)}) async-start(bf16[16,2,8192]{2,1,0:T(2,128)(2,1)} %reshape.290), calls=%async_computation.5 | async-start | bytes 1048576 | tf_op jit(solution)/shard_map/all_to_all | solution.py:85
  189.6 4.8 %convolution_add_fusion.1 = f32[128,2048]{1,0:T(8,128)} fusion(f32[128,2048]{1,0:T(8,128)} %convolution_add_fusion.2, bf16[512,128]{1,0:T(8,128)(2,1)S(1)} %bitcast.153, f32[512,2048]{1,0:T(8,128)} %fusion.35, f32[512]{0:T(512)S(1)} %get-tuple-element.14, f32[512]{0:T(512)S(1)} %get-tuple-element.11, pred[2048]{0:T(1024)(128)(4,1)S(1)} %fusion.27), kind=kOutput, calls=%fused_computation.29 | convolution fusion | flops 273940480 | bytes 6428672 | tf_op jit(solution)/shard_map/hqk,qhc->khc/dot_general | solution.py:29
  194.4 5.8 %all-to-all-done.5 = bf16[16,2,8192]{2,1,0:T(2,128)(2,1)S(1)} async-done(((bf16[16,2,8192]{2,1,0:T(2,128)(2,1)}), bf16[16,2,8192]{2,1,0:T(2,128)(2,1)S(1)}, u32[]{:S(2)}, u32[]{:S(2)}) %all-to-all-start.5) | async-done | bytes 524320 | tf_op jit(solution)/shard_map/all_to_all | solution.py:85
  200.2 3.6 %all-to-all-start.6 = ((bf16[16,2,8192]{2,1,0:T(2,128)(2,1)}), bf16[16,2,8192]{2,1,0:T(2,128)(2,1)S(1)}, u32[]{:S(2)}, u32[]{:S(2)}) async-start(bf16[16,2,8192]{2,1,0:T(2,128)(2,1)} %reshape.292), calls=%async_computation.6 | async-start | bytes 1048576 | tf_op jit(solution)/shard_map/all_to_all | solution.py:86
  203.8 3.7 %fusion.14 = bf16[2048,1,128]{0,2,1:T(8,128)(2,1)S(1)} fusion(f32[128,2048]{1,0:T(8,128)} %convolution_add_fusion.1, bf16[512,128]{1,0:T(8,128)(2,1)S(1)} %bitcast.151, f32[512,2048]{1,0:T(8,128)} %fusion.36, f32[512]{0:T(512)S(1)} %get-tuple-element.15, f32[512]{0:T(512)S(1)} %get-tuple-element.12, pred[2048]{0:T(1024)(128)(4,1)S(1)} %fusion.27), kind=kOutput, calls=%fused_computation.36 | convolution fusion | flops 274202624 | bytes 5904384 | tf_op jit(solution)/shard_map/hqk,qhc->khc/dot_general | solution.py:29
  209.7 4.2 %all-to-all-done.6 = bf16[16,2,8192]{2,1,0:T(2,128)(2,1)S(1)} async-done(((bf16[16,2,8192]{2,1,0:T(2,128)(2,1)}), bf16[16,2,8192]{2,1,0:T(2,128)(2,1)S(1)}, u32[]{:S(2)}, u32[]{:S(2)}) %all-to-all-start.6) | async-done | bytes 524320 | tf_op jit(solution)/shard_map/all_to_all | solution.py:86
  213.9 3.6 %all-to-all-start.7 = ((bf16[16,2,8192]{2,1,0:T(2,128)(2,1)}), bf16[16,2,8192]{2,1,0:T(2,128)(2,1)S(1)}, u32[]{:S(2)}, u32[]{:S(2)}) async-start(bf16[16,2,8192]{2,1,0:T(2,128)(2,1)} %reshape.294), calls=%async_computation.7 | async-start | bytes 1048576 | tf_op jit(solution)/shard_map/all_to_all | solution.py:87
  221.3 6.2 %all-to-all-done.7 = bf16[16,2,8192]{2,1,0:T(2,128)(2,1)S(1)} async-done(((bf16[16,2,8192]{2,1,0:T(2,128)(2,1)}), bf16[16,2,8192]{2,1,0:T(2,128)(2,1)S(1)}, u32[]{:S(2)}, u32[]{:S(2)}) %all-to-all-start.7) | async-done | bytes 524320 | tf_op jit(solution)/shard_map/all_to_all | solution.py:87
  (99 shorter events, 46.1 us)
Async XLA Ops:
  7.2 106.0 %copy-start = (bf16[1,128,3072]{2,1,0:T(8,128)(2,1)S(1)}, bf16[1,128,3072]{2,1,0:T(8,128)(2,1)}, u32[]{:S(2)}) copy-start(bf16[1,128,3072]{2,1,0:T(8,128)(2,1)} %param.9) | copy-start | bytes 2359300
  7.2 24.6 %copy-start.12 = (bf16[1,128,2048]{2,1,0:T(8,128)(2,1)S(1)}, bf16[1,128,2048]{2,1,0:T(8,128)(2,1)}, u32[]{:S(2)}) copy-start(bf16[1,128,2048]{2,1,0:T(8,128)(2,1)} %param.7) | copy-start | bytes 1572868
  7.2 39.1 %copy-start.13 = (bf16[1,128,2048]{2,1,0:T(8,128)(2,1)S(1)}, bf16[1,128,2048]{2,1,0:T(8,128)(2,1)}, u32[]{:S(2)}) copy-start(bf16[1,128,2048]{2,1,0:T(8,128)(2,1)} %param.8) | copy-start | bytes 1572868
  7.2 106.0 %all-gather.2.cloned.1.call-start = ((), (), s32[]{:S(2)}) async-start(), calls=%async_computation.8 | async-start | bytes 12976128 | tf_op jit(solution)/shard_map/all_gather | solution.py:71
  28.0 14.0 %all-to-all-start = ((bf16[128,16,128]{0,2,1:T(8,128)(2,1)}), bf16[128,16,128]{0,2,1:T(8,128)(2,1)S(1)}, u32[]{:S(2)}, u32[]{:S(2)}) async-start(bf16[128,16,128]{0,2,1:T(8,128)(2,1)} %bitcast.1), calls=%async_computation | async-start | bytes 1048576 | tf_op jit(solution)/shard_map/all_to_all | solution.py:76
  42.0 13.6 %all-to-all-start.1 = ((bf16[128,16,128]{0,2,1:T(8,128)(2,1)}), bf16[128,16,128]{0,2,1:T(8,128)(2,1)S(1)}, u32[]{:S(2)}, u32[]{:S(2)}) async-start(bf16[128,16,128]{0,2,1:T(8,128)(2,1)} %bitcast.5), calls=%async_computation.1 | async-start | bytes 1048576 | tf_op jit(solution)/shard_map/all_to_all | solution.py:77
  47.5 17.4 %copy-start.10 = (bf16[4,128,1,128]{3,1,0,2:T(8,128)(2,1)}, bf16[4,128,1,128]{3,1,0,2:T(8,128)(2,1)S(1)}, u32[]{:S(2)}) copy-start(bf16[4,128,1,128]{3,1,0,2:T(8,128)(2,1)S(1)} %copy.104) | copy-start | bytes 393220
  47.9 17.0 %copy-start.8 = (bf16[4,128,1,128]{3,1,0,2:T(8,128)(2,1)}, bf16[4,128,1,128]{3,1,0,2:T(8,128)(2,1)S(1)}, u32[]{:S(2)}) copy-start(bf16[4,128,1,128]{3,1,0,2:T(8,128)(2,1)S(1)} %copy.94) | copy-start | bytes 393220
  55.7 64.9 %all-to-all-start.4 = ((bf16[128,16,128]{0,2,1:T(8,128)(2,1)}), bf16[128,16,128]{0,2,1:T(8,128)(2,1)S(1)}, u32[]{:S(2)}, u32[]{:S(2)}) async-start(bf16[128,16,128]{0,2,1:T(8,128)(2,1)} %bitcast.17), calls=%async_computation.4 | async-start | bytes 1048576 | tf_op jit(solution)/shard_map/all_to_all | solution.py:78
  120.6 18.9 %all-to-all-start.3 = ((bf16[128,16,128]{0,2,1:T(8,128)(2,1)}), bf16[128,16,128]{0,2,1:T(8,128)(2,1)S(1)}, u32[]{:S(2)}, u32[]{:S(2)}) async-start(bf16[128,16,128]{0,2,1:T(8,128)(2,1)} %copy.98), calls=%async_computation.3 | async-start | bytes 1048576 | tf_op jit(solution)/shard_map/all_to_all | solution.py:79
  139.8 3.8 %copy-start.2 = (f32[512,2048]{1,0:T(8,128)S(1)}, f32[512,2048]{1,0:T(8,128)}, u32[]{:S(2)}) copy-start(f32[512,2048]{1,0:T(8,128)} %get-tuple-element.33) | copy-start | bytes 12582916
  139.8 6.0 %copy-start.14 = (bf16[4,128,1,128]{3,1,0,2:T(8,128)(2,1)}, bf16[4,128,1,128]{3,1,0,2:T(8,128)(2,1)S(1)}, u32[]{:S(2)}) copy-start(bf16[4,128,1,128]{3,1,0,2:T(8,128)(2,1)S(1)} %get-tuple-element.23) | copy-start | bytes 393220
  139.8 13.6 %copy-start.18 = (bf16[4,128,1,128]{3,1,0,2:T(8,128)(2,1)}, bf16[4,128,1,128]{3,1,0,2:T(8,128)(2,1)S(1)}, u32[]{:S(2)}) copy-start(bf16[4,128,1,128]{3,1,0,2:T(8,128)(2,1)S(1)} %get-tuple-element.25) | copy-start | bytes 393220
  139.8 18.0 %copy-start.16 = (bf16[4,128,1,128]{3,1,0,2:T(8,128)(2,1)}, bf16[4,128,1,128]{3,1,0,2:T(8,128)(2,1)S(1)}, u32[]{:S(2)}) copy-start(bf16[4,128,1,128]{3,1,0,2:T(8,128)(2,1)S(1)} %get-tuple-element.24) | copy-start | bytes 393220
  140.6 17.3 %copy-start.6 = (f32[512,2048]{1,0:T(8,128)}, f32[512,2048]{1,0:T(8,128)S(1)}, u32[]{:S(2)}) copy-start(f32[512,2048]{1,0:T(8,128)S(1)} %fusion.37) | copy-start | bytes 12582916
  143.6 3.8 %copy-start.4 = (f32[512,2048]{1,0:T(8,128)S(1)}, f32[512,2048]{1,0:T(8,128)}, u32[]{:S(2)}) copy-start(f32[512,2048]{1,0:T(8,128)} %fusion.36) | copy-start | bytes 12582916
  143.6 5.0 %copy-start.5 = (f32[512,2048]{1,0:T(8,128)S(1)}, f32[512,2048]{1,0:T(8,128)}, u32[]{:S(2)}) copy-start(f32[512,2048]{1,0:T(8,128)} %fusion.35) | copy-start | bytes 12582916
  165.3 9.0 %copy-start.9 = (bf16[4,128,1,128]{3,1,0,2:T(8,128)(2,1)S(1)}, bf16[4,128,1,128]{3,1,0,2:T(8,128)(2,1)}, u32[]{:S(2)}) copy-start(bf16[4,128,1,128]{3,1,0,2:T(8,128)(2,1)} %copy-done.8) | copy-start | bytes 393220
  181.0 8.6 %copy-start.17 = (bf16[4,128,1,128]{3,1,0,2:T(8,128)(2,1)S(1)}, bf16[4,128,1,128]{3,1,0,2:T(8,128)(2,1)}, u32[]{:S(2)}) copy-start(bf16[4,128,1,128]{3,1,0,2:T(8,128)(2,1)} %copy-done.16) | copy-start | bytes 393220
  186.0 14.2 %all-to-all-start.5 = ((bf16[16,2,8192]{2,1,0:T(2,128)(2,1)}), bf16[16,2,8192]{2,1,0:T(2,128)(2,1)S(1)}, u32[]{:S(2)}, u32[]{:S(2)}) async-start(bf16[16,2,8192]{2,1,0:T(2,128)(2,1)} %reshape.290), calls=%async_computation.5 | async-start | bytes 1048576 | tf_op jit(solution)/shard_map/all_to_all | solution.py:85
  189.6 14.2 %copy-start.15 = (bf16[4,128,1,128]{3,1,0,2:T(8,128)(2,1)S(1)}, bf16[4,128,1,128]{3,1,0,2:T(8,128)(2,1)}, u32[]{:S(2)}) copy-start(bf16[4,128,1,128]{3,1,0,2:T(8,128)(2,1)} %copy-done.14) | copy-start | bytes 393220
  200.2 13.6 %all-to-all-start.6 = ((bf16[16,2,8192]{2,1,0:T(2,128)(2,1)}), bf16[16,2,8192]{2,1,0:T(2,128)(2,1)S(1)}, u32[]{:S(2)}, u32[]{:S(2)}) async-start(bf16[16,2,8192]{2,1,0:T(2,128)(2,1)} %reshape.292), calls=%async_computation.6 | async-start | bytes 1048576 | tf_op jit(solution)/shard_map/all_to_all | solution.py:86
  213.9 13.6 %all-to-all-start.7 = ((bf16[16,2,8192]{2,1,0:T(2,128)(2,1)}), bf16[16,2,8192]{2,1,0:T(2,128)(2,1)S(1)}, u32[]{:S(2)}, u32[]{:S(2)}) async-start(bf16[16,2,8192]{2,1,0:T(2,128)(2,1)} %reshape.294), calls=%async_computation.7 | async-start | bytes 1048576 | tf_op jit(solution)/shard_map/all_to_all | solution.py:87
  219.4 10.0 %copy-start.1 = (bf16[1,128,3072]{2,1,0:T(8,128)(2,1)S(1)}, bf16[1,128,3072]{2,1,0:T(8,128)(2,1)}, u32[]{:S(2)}) copy-start(bf16[1,128,3072]{2,1,0:T(8,128)(2,1)} %param.9) | copy-start | bytes 2359300
  (5 other events, 9.0 us)
Sparse Core Ops, SparseCore 0:
  26.1 87.0 all-gather.1
where the time goes:
time: 237 us; the launch traced here: 236 us
  waiting for transfers between devices  84.8 us (36%)
  matrix products  52.5 us (22%)
  starting transfers between devices  28.6 us (12%)
  local copies, waits for them, and re-layouts  23.3 us (10%)
  blocking collectives  16.7 us (7%)
  other arithmetic  15.3 us (6%)
  between operations  15.2 us (6%)
    all_gather x1, waiting for transfers between devices, per_device(): lax.all_gather(stream_rows, 'seq', axis=1, tiled=True)  45.6 us
    unnamed x58, local copies, waits for them, and re-layouts  17.8 us
    all_to_all x1, blocking collectives, per_device(): lax.all_to_all(outgoing, 'dp', split_axis=0, concat_axis=0, tiled=True)  16.7 us
    dot_general x4, matrix products, attention_grads(): jnp.einsum('qhc,khc->hqk', grad_block, value_heads, preferred_element_typ...  16.4 us
    dot_general x4, matrix products, attention_grads(): jnp.einsum('hqk,qhc->khc', attention.astype(jnp.bfloat16), grad_block, pr...  13 us
    dot_general x4, matrix products, attention_grads(): jnp.einsum('qhc,khc->hqk', query_block, key_heads, preferred_element_type...  10.7 us
    all_to_all x1, waiting for transfers between devices, per_device(): lax.all_to_all(by_heads(query_rows), 'dp', split_axis=1, concat_axis=0, t...  9.29 us
    convert_element_type x1, other arithmetic, attention_grads(): (attention * (weight_grad - row_dot) * factor).astype(jnp.bfloat16)  8.21 us
  transfers between devices with their start and end apart: 8, of which 7 were waited for; matrix products, arithmetic and copies ran while one was open for 17% of the time, Pallas kernels for 0%

commit v1 on v0

--- a/solution.py
+++ b/solution.py
@@ -68,7 +68,9 @@
     projected = jnp.einsum(
         "te,kre->tkr",
         out_grad[0],
-        lax.all_gather(stream_rows, "seq", axis=1, tiled=True),
+        jnp.concatenate(
+            lax.all_to_all(jnp.stack([stream_rows] * lax.axis_size("seq")), "seq", 0, 0), axis=1
+        ),
         preferred_element_type=jnp.float32,
     )
     grad_tokens = projected.astype(jnp.bfloat16)

time: 237 us -> 780 us (3.29)
  waiting for transfers between devices: 84.8 us -> 570 us
  local copies, waits for them, and re-layouts: 23.3 us -> 64.6 us
  starting transfers between devices: 28.6 us -> 51.4 us
  between operations: 15.2 us -> 1.81 us
    all_to_all x1 -> x2, waiting for transfers between devices: 9.29 us -> 547 us  [the longest x1 539 us: per_device(): lax.all_to_all(jnp.stack([stream_rows] * lax.axis_size('seq')), 'seq', 0, 0)]
    all_gather x1 -> x0, waiting for transfers between devices: 45.6 us -> none  [per_device(): lax.all_gather(stream_rows, 'seq', axis=1, tiled=True)]
    reshape x0 -> x2, local copies, waits for them, and re-layouts: none -> 31.4 us  [per_device(): jnp.concatenate(lax.all_to_all(jnp.stack([stream_rows] * lax.axis_size('s...]
    all_to_all x1 -> x2, starting transfers between devices: 3.71 us -> 22.6 us  [the longest x1 15.5 us: per_device(): lax.all_to_all(jnp.stack([stream_rows] * lax.axis_size('seq')), 'seq', 0, 0)]
    unnamed x58 -> x66, local copies, waits for them, and re-layouts: 17.8 us -> 22.4 us
  transfers between devices with their start and end apart: 8 -> 8, of which waited for: 7 -> 6; matrix products, arithmetic and copies ran while one was open for 17% -> 13% of each run, Pallas kernels for 0% -> 0%
where the time goes in v1:
time: 780 us; the launch traced here: 778 us
  waiting for transfers between devices  570 us (73%)
  local copies, waits for them, and re-layouts  64.6 us (8%)
  matrix products  59.4 us (8%)
  starting transfers between devices  51.4 us (7%)
  other arithmetic  17 us (2%)
  blocking collectives  13.3 us (2%)
    all_to_all x1, waiting for transfers between devices, per_device(): lax.all_to_all(jnp.stack([stream_rows] * lax.axis_size('seq')), 'seq', 0, 0)  539 us
    reshape x2, local copies, waits for them, and re-layouts, per_device(): jnp.concatenate(lax.all_to_all(jnp.stack([stream_rows] * lax.axis_size('s...  31.4 us
    unnamed x66, local copies, waits for them, and re-layouts  22.4 us
    dot_general x4, matrix products, attention_grads(): jnp.einsum('qhc,khc->hqk', grad_block, value_heads, preferred_element_typ...  21.6 us
  transfers between devices with their start and end apart: 8, of which 6 were waited for; matrix products, arithmetic and copies ran while one was open for 13% of the time, Pallas kernels for 0%

profile of v1, /device:TPU:32, one launch (start us, length us, event | category | flops | bytes accessed | tf_op | source)
XLA Modules:
  0.0 777.9 jit_solution(3538668867452895307)
XLA Ops:
  2.5 7.0 all-to-all-start.2
  11.5 7.8 all-to-all-done.2
  19.3 3.7 all-to-all-start.1
  24.4 9.0 %all-to-all-done.1 = bf16[128,16,128]{0,2,1:T(8,128)(2,1)S(1)} async-done(((bf16[128,16,128]{0,2,1:T(8,128)(2,1)}), bf16[128,16,128]{0,2,1:T(8,128)(2,1)S(1)}, u32[]{:S(2)}, u32[]{:S(2)}) %all-to-all-start.1) | async-done | bytes 524320 | tf_op jit(solution)/shard_map/all_to_all | solution.py:79
  33.3 13.3 %all_to_all.115 = bf16[128,16,128]{0,2,1:T(8,128)(2,1)S(1)} all-to-all(bf16[128,16,128]{0,2,1:T(8,128)(2,1)S(1)} %bitcast.140), channel_id=1, replica_groups=mesh['dp'=16,'seq'=32] {'dp'}, dimensions={1} | all-to-all | bytes 1048576 | tf_op jit(solution)/shard_map/all_to_all | solution.py:78
  46.7 6.8 stack.2
  53.5 15.5 %all-to-all-start.3 = ((bf16[32,16,4,3072]{3,2,1,0:T(4,128)(2,1)}), bf16[32,16,4,3072]{3,2,1,0:T(4,128)(2,1)}, u32[]{:S(2)}, u32[]{:S(2)}) async-start(bf16[32,16,4,3072]{3,2,1,0:T(4,128)(2,1)} %stack.2), calls=%async_computation.3 | async-start | bytes 25165824 | tf_op jit(solution)/shard_map/all_to_all | solution.py:72
  79.7 539.1 %all-to-all-done.3 = bf16[32,16,4,3072]{3,2,1,0:T(4,128)(2,1)} async-done(((bf16[32,16,4,3072]{3,2,1,0:T(4,128)(2,1)}), bf16[32,16,4,3072]{3,2,1,0:T(4,128)(2,1)}, u32[]{:S(2)}, u32[]{:S(2)}) %all-to-all-start.3) | async-done | bytes 12582944 | tf_op jit(solution)/shard_map/all_to_all | solution.py:72
  618.8 3.6 all-to-all-start.5
  622.3 11.3 %copy.76 = bf16[16,32,4,3072]{3,2,1,0:T(4,128)(2,1)} copy(bf16[16,32,4,3072]{3,2,0,1:T(4,128)(2,1)} %bitcast.11) | data formatting | bytes 25165824 | tf_op jit(solution)/shard_map/reshape | solution.py:71
  633.6 20.2 %reshape.287 = bf16[16,128,3072]{2,1,0:T(8,128)(2,1)} reshape(bf16[16,32,4,3072]{3,2,1,0:T(4,128)(2,1)} %copy.76) | data formatting | bytes 25165824 | tf_op jit(solution)/shard_map/reshape | solution.py:71
  653.8 7.2 fusion.21
  661.0 7.2 all-to-all-start.4
  674.3 4.9 all-to-all-done.4
  679.4 4.6 fusion.19
  686.9 3.9 multiply_reduce_fusion.3
  699.4 4.4 multiply_reduce_fusion.2
  709.1 3.8 all-to-all-start.8
  712.9 10.6 %multiply_reduce_fusion.1 = (f32[512]{0:T(512)S(1)}, f32[512]{0:T(512)S(1)}, bf16[512,2048]{1,0:T(8,128)(2,1)S(1)}, f32[512,2048]{1,0:T(8,128)}) fusion(f32[512]{0:T(512)S(1)} %get-tuple-element.11, f32[512]{0:T(512)S(1)} %get-tuple-element.8, f32[512,2048]{1,0:T(8,128)} %fusion.35, pred[2048]{0:T(1024)(128)(4,1)S(1)} %fusion.27, f32[512,2048]{1,0:T(8,128)} %fusion.37, ...), kind=kOutput, calls=%fused_computation.5 | convolution fusion | flops 289405952 | bytes 27938816 | tf_op jit(solution)/shard_map/qhc,khc->hqk/dot_general | solution.py:35
  725.9 7.3 multiply_convert_fusion.3
  745.2 7.0 all-to-all-start.7
  757.2 5.2 all-to-all-done.7
  762.4 3.6 all-to-all-start.6
  771.6 4.5 all-to-all-done.6
  (110 shorter events, 64.7 us)
Async XLA Ops:
  0.6 653.2 %copy-start = (bf16[1,128,3072]{2,1,0:T(8,128)(2,1)S(1)}, bf16[1,128,3072]{2,1,0:T(8,128)(2,1)}, u32[]{:S(2)}) copy-start(bf16[1,128,3072]{2,1,0:T(8,128)(2,1)} %param.9) | copy-start | bytes 2359300
  2.5 16.9 %all-to-all-start.2 = ((bf16[16,4,3072]{2,1,0:T(4,128)(2,1)}), bf16[16,4,3072]{2,1,0:T(4,128)(2,1)S(1)}, u32[]{:S(2)}, u32[]{:S(2)}) async-start(bf16[16,4,3072]{2,1,0:T(4,128)(2,1)} %broadcast_select_fusion), calls=%async_computation.2 | async-start | bytes 786432 | tf_op jit(solution)/shard_map/all_to_all | solution.py:67
  19.3 14.0 %all-to-all-start.1 = ((bf16[128,16,128]{0,2,1:T(8,128)(2,1)}), bf16[128,16,128]{0,2,1:T(8,128)(2,1)S(1)}, u32[]{:S(2)}, u32[]{:S(2)}) async-start(bf16[128,16,128]{0,2,1:T(8,128)(2,1)} %bitcast.5), calls=%async_computation.1 | async-start | bytes 1048576 | tf_op jit(solution)/shard_map/all_to_all | solution.py:79
  53.5 16.2 %copy-start.22 = (bf16[1,128,2048]{2,1,0:T(8,128)(2,1)S(1)}, bf16[1,128,2048]{2,1,0:T(8,128)(2,1)}, u32[]{:S(2)}) copy-start(bf16[1,128,2048]{2,1,0:T(8,128)(2,1)} %param.8) | copy-start | bytes 1572868
  53.5 565.3 %all-to-all-start.3 = ((bf16[32,16,4,3072]{3,2,1,0:T(4,128)(2,1)}), bf16[32,16,4,3072]{3,2,1,0:T(4,128)(2,1)}, u32[]{:S(2)}, u32[]{:S(2)}) async-start(bf16[32,16,4,3072]{3,2,1,0:T(4,128)(2,1)} %stack.2), calls=%async_computation.3 | async-start | bytes 25165824 | tf_op jit(solution)/shard_map/all_to_all | solution.py:72
  71.2 5.9 copy-start.18
  71.3 5.7 copy-start.16
  71.6 596.6 %copy-start.20 = (bf16[4,128,1,128]{3,1,0,2:T(8,128)(2,1)}, bf16[4,128,1,128]{3,1,0,2:T(8,128)(2,1)S(1)}, u32[]{:S(2)}) copy-start(bf16[4,128,1,128]{3,1,0,2:T(8,128)(2,1)S(1)} %copy.84) | copy-start | bytes 393220
  618.8 42.3 %all-to-all-start.5 = ((bf16[128,16,128]{0,2,1:T(8,128)(2,1)}), bf16[128,16,128]{0,2,1:T(8,128)(2,1)S(1)}, u32[]{:S(2)}, u32[]{:S(2)}) async-start(bf16[128,16,128]{0,2,1:T(8,128)(2,1)} %bitcast.18), calls=%async_computation.5 | async-start | bytes 1048576 | tf_op jit(solution)/shard_map/all_to_all | solution.py:80
  661.0 18.2 %all-to-all-start.4 = ((bf16[128,16,128]{0,2,1:T(8,128)(2,1)}), bf16[128,16,128]{0,2,1:T(8,128)(2,1)S(1)}, u32[]{:S(2)}, u32[]{:S(2)}) async-start(bf16[128,16,128]{0,2,1:T(8,128)(2,1)} %fusion.21), calls=%async_computation.4 | async-start | bytes 1048576 | tf_op jit(solution)/shard_map/all_to_all | solution.py:81
  679.4 6.3 copy-start.8
  679.4 7.5 copy-start.11
  690.8 22.1 %copy-start.23 = (f32[512]{0:T(512)}, f32[512]{0:T(512)S(1)}, u32[]{:S(2)}) copy-start(f32[512]{0:T(512)S(1)} %get-tuple-element.8) | copy-start | bytes 6148
  690.8 22.1 %copy-start.24 = (f32[512]{0:T(512)}, f32[512]{0:T(512)S(1)}, u32[]{:S(2)}) copy-start(f32[512]{0:T(512)S(1)} %get-tuple-element.9) | copy-start | bytes 6148
  709.1 36.1 %all-to-all-start.8 = ((bf16[16,2,8192]{2,1,0:T(2,128)(2,1)}), bf16[16,2,8192]{2,1,0:T(2,128)(2,1)S(1)}, u32[]{:S(2)}, u32[]{:S(2)}) async-start(bf16[16,2,8192]{2,1,0:T(2,128)(2,1)} %reshape.304), calls=%async_computation.8 | async-start | bytes 1048576 | tf_op jit(solution)/shard_map/all_to_all | solution.py:89
  712.9 10.6 %copy-start.3 = (f32[512,2048]{1,0:T(8,128)S(1)}, f32[512,2048]{1,0:T(8,128)}, u32[]{:S(2)}) copy-start(f32[512,2048]{1,0:T(8,128)} %get-tuple-element.30) | copy-start | bytes 12582916
  712.9 10.6 %copy-start.10 = (f32[512,2048]{1,0:T(8,128)S(1)}, f32[512,2048]{1,0:T(8,128)}, u32[]{:S(2)}) copy-start(f32[512,2048]{1,0:T(8,128)} %fusion.35) | copy-start | bytes 12582916
  712.9 13.0 %copy-start.13 = (f32[512,2048]{1,0:T(8,128)S(1)}, f32[512,2048]{1,0:T(8,128)}, u32[]{:S(2)}) copy-start(f32[512,2048]{1,0:T(8,128)} %fusion.36) | copy-start | bytes 12582916
  723.5 10.5 %copy-start.14 = (bf16[512,2048]{1,0:T(8,128)(2,1)}, bf16[512,2048]{1,0:T(8,128)(2,1)S(1)}, u32[]{:S(2)}) copy-start(bf16[512,2048]{1,0:T(8,128)(2,1)S(1)} %get-tuple-element.28) | copy-start | bytes 6291460
  725.9 7.4 copy-start.19
  742.8 11.8 %copy-start.15 = (bf16[512,2048]{1,0:T(8,128)(2,1)S(1)}, bf16[512,2048]{1,0:T(8,128)(2,1)}, u32[]{:S(2)}) copy-start(bf16[512,2048]{1,0:T(8,128)(2,1)} %copy-done.14) | copy-start | bytes 6291460
  745.2 17.2 %all-to-all-start.7 = ((bf16[16,2,8192]{2,1,0:T(2,128)(2,1)}), bf16[16,2,8192]{2,1,0:T(2,128)(2,1)}, u32[]{:S(2)}, u32[]{:S(2)}) async-start(bf16[16,2,8192]{2,1,0:T(2,128)(2,1)} %reshape.302), calls=%async_computation.7 | async-start | bytes 1048576 | tf_op jit(solution)/shard_map/all_to_all | solution.py:88
  762.4 13.6 %all-to-all-start.6 = ((bf16[16,2,8192]{2,1,0:T(2,128)(2,1)}), bf16[16,2,8192]{2,1,0:T(2,128)(2,1)S(1)}, u32[]{:S(2)}, u32[]{:S(2)}) async-start(bf16[16,2,8192]{2,1,0:T(2,128)(2,1)} %reshape.300), calls=%async_computation.6 | async-start | bytes 1048576 | tf_op jit(solution)/shard_map/all_to_all | solution.py:87
  767.9 10.0 %copy-start.1 = (bf16[1,128,3072]{2,1,0:T(8,128)(2,1)S(1)}, bf16[1,128,3072]{2,1,0:T(8,128)(2,1)}, u32[]{:S(2)}) copy-start(bf16[1,128,3072]{2,1,0:T(8,128)(2,1)} %param.9) | copy-start | bytes 2359300
  (9 other events, 26.5 us)
